TPU v7x, 32 devices: a whole 2x2x4 slice. The times are simulated.
32 devices in a mesh: group: 16 (over z, x, core), loop: 2 (over y).
Axes of the slice: x: 2, y: 2, z: 4, core: 2. Of those that a mesh axis runs over, the one named last changes fastest.
Arguments:
- user_factors: bfloat16 [32768, 256], P('group'), may hold values from -1.5 to 1.5
- item_factors: bfloat16 [2048, 256], P('loop'), may hold values from -1.5 to 1.5
- tag_factors: bfloat16 [2048, 256], P('group'), may hold values from -1.5 to 1.5
- ratings: bfloat16 [32768, 2048], P('group', 'loop'), may hold values from -6 to 6
- rating_tiles: int32 [256, 16], P('group', 'loop'), may hold values 0 or 1
- tag_links: bfloat16 [2048, 2048], P('loop', 'group'), may hold values from -6 to 6
- link_tiles: int32 [16, 16], P('loop', 'group'), may hold values 0 or 1
Outputs:
- new_users: bfloat16 [32768, 256], P('group')
- new_items: bfloat16 [2048, 256], P('loop')
- new_tags: bfloat16 [2048, 256], P('group')
Inputs may be any that keep to these rules, and one draw needn't show every extreme that they name: `rating_tiles`: 1 marks a tile of observed entries, 0 an empty tile. `link_tiles`: 1 marks a tile of observed entries, 0 an empty tile.
All inputs are finite; a program needn't handle non-finite values. No bound on the sum of `rating_tiles` or of `link_tiles` on one device may be relied on, other than what follows from the above.
Results may differ from a plain program's by a relative error of at most 0.0034.
Values may be sent and summed in bfloat16 or wider, within the bound.
No kernel may reach another device: no remote copies, remote signals or barrier semaphores. Data moves between devices by JAX's collectives and lax.ppermute only.
A program may use at most 64 MiB of HBM per device.

v0:
```python
import jax
import jax.numpy as jnp
from jax import lax
from jax.sharding import PartitionSpec as P

step_users = 0.015
step_items = 0.004
step_tags = 0.015


def tile_masked(values, tile_flags):
    height, breadth = values.shape
    blocks = values.reshape(height // 128, 128, breadth // 128, 128)
    masked = blocks * tile_flags.astype(jnp.float32)[:, None, :, None]
    return masked.reshape(height, breadth)


def residual_of(observed, row_factors, column_factors, tile_flags):
    predicted = lax.dot_general(
        row_factors, column_factors, (((1,), (1,)), ((), ())), preferred_element_type=jnp.float32
    )
    return tile_masked(observed.astype(jnp.float32) - predicted, tile_flags).astype(jnp.bfloat16)


def transposed_product(first_operand, second_operand):
    return lax.dot_general(
        first_operand, second_operand, (((0,), (0,)), ((), ())), preferred_element_type=jnp.float32
    )


def advance(factors, gradient, rate):
    return (factors.astype(jnp.float32) + rate * gradient).astype(jnp.bfloat16)


def own_share(factors, axis_count, position):
    share_rows = factors.shape[0] // axis_count
    return lax.dynamic_slice_in_dim(factors, position * share_rows, share_rows, 0)


def shards(user_factors, item_factors, tag_factors, ratings, rating_tiles, tag_links, link_tiles):
    link_errors = residual_of(tag_links, item_factors, tag_factors, link_tiles)
    rating_errors = residual_of(ratings, user_factors, item_factors, rating_tiles)
    item_part = transposed_product(rating_errors, user_factors) + jnp.dot(
        link_errors, tag_factors, preferred_element_type=jnp.float32
    )
    user_part = jnp.dot(rating_errors, item_factors, preferred_element_type=jnp.float32)
    tag_part = transposed_product(link_errors, item_factors)
    item_share = lax.psum_scatter(item_part, "group", scatter_dimension=0, tiled=True)
    group_count = lax.axis_size("group")
    group_position = lax.axis_index("group")
    fresh_share = advance(
        own_share(item_factors, group_count, group_position), item_share, step_items
    )
    new_items = lax.all_gather(fresh_share, "group", axis=0, tiled=True)
    user_grad, tag_grad = lax.psum((user_part, tag_part), "loop")
    new_users = advance(user_factors, user_grad, step_users)
    new_tags = advance(tag_factors, tag_grad, step_tags)
    return (new_users, new_items, new_tags)


def solution(mesh):
    in_specs = (
        P("group", None),
        P("loop", None),
        P("group", None),
        P("group", "loop"),
        P("group", "loop"),
        P("loop", "group"),
        P("loop", "group"),
    )
    out_specs = (P("group", None), P("loop", None), P("group", None))
    return jax.shard_map(shards, mesh=mesh, in_specs=in_specs, out_specs=out_specs, check_vma=False)
```

profile of v0, /device:TPU:0, one launch (start us, length us, event | category | flops | bytes accessed | tf_op | source)
XLA Modules:
  0.0 111.5 jit_solution(9205640242450746977)
XLA Ops:
  8.0 0.0 reduce-scatter.2.cloned.1.call-start
  8.0 0.7 convert_element_type.38
  8.7 0.1 copy.10
  8.8 0.7 convert_bitcast_fusion
  9.5 0.1 broadcast_bitcast_fusion
  9.5 0.0 copy-start
  9.5 0.0 copy-start.1
  9.5 0.0 copy-start.2
  9.5 0.6 mul.49
  10.2 0.4 copy-done
  10.6 0.3 copy-done.1
  10.9 1.3 %copy-done.2 = bf16[2048,1024]{1,0:T(8,128)(2,1)S(1)} copy-done((bf16[2048,1024]{1,0:T(8,128)(2,1)S(1)}, bf16[2048,1024]{1,0:T(8,128)(2,1)}, u32[]{:S(2)}) %copy-start.2) | copy-done | bytes 4194328
  12.2 2.0 %fusion = bf16[2048,1024]{1,0:T(8,128)(2,1)S(1)} fusion(f32[256,8,8,128]{3,2,1,0:T(8,128)S(1)} %bitcast.22, bf16[2048,1024]{1,0:T(8,128)(2,1)S(1)} %copy-done.2, bf16[2048,256]{1,0:T(8,128)(2,1)S(1)} %copy-done.1, bf16[1024,256]{1,0:T(8,128)(2,1)S(1)} %copy-done), kind=kOutput, calls=%fused_computation.1 | convolution fusion | flops 1082130432 | bytes 18350080 | tf_op jit(solution)/shard_map/dot_general | solution.py:19
  14.3 0.0 copy-start.3
  14.3 0.0 copy-start.4
  14.3 0.0 copy-start.5
  14.3 1.3 %fusion.4 = f32[1024,256]{1,0:T(8,128)S(1)} fusion(bf16[2048,1024]{1,0:T(8,128)(2,1)S(1)} %fusion, bf16[2048,256]{1,0:T(8,128)(2,1)S(1)} %copy-done.1), kind=kOutput, calls=%fused_computation.12 | convolution fusion | flops 1073741824 | bytes 6291456 | tf_op jit(solution)/shard_map/dot_general | solution.py:26
  15.6 0.6 copy-done.3
  16.2 0.0 copy-done.4
  16.2 0.0 copy-done.5
  16.2 0.3 fusion.2
  16.5 1.2 %convolution_add_fusion = f32[1024,256]{1,0:T(8,128)} fusion(f32[1024,256]{1,0:T(8,128)S(1)} %fusion.4, bf16[1024,128]{1,0:T(8,128)(2,1)S(1)} %fusion.2, bf16[128,256]{1,0:T(8,128)(2,1)S(1)} %copy-done.4), kind=kOutput, calls=%fused_computation.3 | convolution fusion | flops 67371008 | bytes 2424832 | tf_op jit(solution)/shard_map/dot_general | solution.py:43
  17.8 0.0 reduce-scatter.2.cloned.1.call-update
  17.8 0.0 all-reduce.3.cloned.1.call-start
  17.9 0.9 fusion.5
  18.8 4.8 %fusion.3 = f32[2048,256]{1,0:T(8,128)} fusion(bf16[2048,1024]{1,0:T(8,128)(2,1)} %copy-done.3, bf16[1024,256]{1,0:T(8,128)(2,1)S(1)} %copy-done), kind=kOutput, calls=%fused_computation.11 | convolution fusion | flops 1073741824 | bytes 6815744 | tf_op jit(solution)/shard_map/dot_general | solution.py:46
  23.5 0.0 all-reduce.3.cloned.1.call-update
  23.6 54.4 %reduce-scatter.2.cloned.1.call-done = f32[64,256]{1,0:T(8,128)} async-done(((f32[1024,256]{1,0:T(8,128)}), f32[64,256]{1,0:T(8,128)}) %reduce-scatter.2.cloned.1.call-update) | async-done | bytes 65552 | tf_op jit(solution)/shard_map/reduce_scatter | solution.py:48
  78.0 0.9 add_convert_fusion.2
  78.8 20.9 %all_gather.3 = bf16[1024,256]{1,0:T(8,128)(2,1)S(1)} all-gather(bf16[64,256]{1,0:T(8,128)(2,1)S(1)} %add_convert_fusion.2), channel_id=1, replica_groups=mesh['group'=16,'loop'=2] {'group'}, dimensions={0}, use_global_device_ids=true | all-gather | bytes 557056 | tf_op jit(solution)/shard_map/all_gather | solution.py:54
  99.7 0.0 all-reduce.3.cloned.1.call-done
  99.7 0.0 copy-start.6
  99.7 2.9 %add_convert_fusion = bf16[2048,256]{1,0:T(8,128)(2,1)} fusion(f32[2048,256]{1,0:T(8,128)} %get-tuple-element.3, bf16[2048,256]{1,0:T(8,128)(2,1)S(1)} %copy-done.1), kind=kLoop, calls=%fused_computation.2 | loop fusion | flops 2097152 | bytes 4194304 | tf_op jit(solution)/shard_map/convert_element_type | solution.py:32
  102.6 0.0 copy-done.6
  102.6 0.7 add_convert_fusion.1
  103.3 0.8 copy.16
Async XLA Ops:
  8.0 70.0 %reduce-scatter.2.cloned.1.call-start = ((), (), s32[]{:S(2)}) async-start(), calls=%async_computation.1 | async-start | bytes 1114112 | tf_op jit(solution)/shard_map/reduce_scatter | solution.py:48
  9.5 1.0 copy-start
  9.5 1.4 %copy-start.1 = (bf16[2048,256]{1,0:T(8,128)(2,1)S(1)}, bf16[2048,256]{1,0:T(8,128)(2,1)}, u32[]{:S(2)}) copy-start(bf16[2048,256]{1,0:T(8,128)(2,1)} %param.7) | copy-start | bytes 3145732
  9.5 2.7 %copy-start.2 = (bf16[2048,1024]{1,0:T(8,128)(2,1)S(1)}, bf16[2048,1024]{1,0:T(8,128)(2,1)}, u32[]{:S(2)}) copy-start(bf16[2048,1024]{1,0:T(8,128)(2,1)} %param.10) | copy-start | bytes 12582916
  14.3 1.9 %copy-start.3 = (bf16[2048,1024]{1,0:T(8,128)(2,1)}, bf16[2048,1024]{1,0:T(8,128)(2,1)S(1)}, u32[]{:S(2)}) copy-start(bf16[2048,1024]{1,0:T(8,128)(2,1)S(1)} %fusion) | copy-start | bytes 12582916
  14.3 1.9 %copy-start.4 = (bf16[128,256]{1,0:T(8,128)(2,1)S(1)}, bf16[128,256]{1,0:T(8,128)(2,1)}, u32[]{:S(2)}) copy-start(bf16[128,256]{1,0:T(8,128)(2,1)} %param.9) | copy-start | bytes 196612
  14.3 1.9 %copy-start.5 = (bf16[1024,128]{1,0:T(8,128)(2,1)S(1)}, bf16[1024,128]{1,0:T(8,128)(2,1)}, u32[]{:S(2)}) copy-start(bf16[1024,128]{1,0:T(8,128)(2,1)} %param.12) | copy-start | bytes 786436
  17.8 81.9 %all-reduce.3.cloned.1.call-start = ((), (), s32[]{:S(2)}) async-start(), calls=%async_computation.2 | async-start | bytes 4456448 | tf_op jit(solution)/shard_map/psum | solution.py:55
  99.7 2.9 %copy-start.6 = (f32[128,256]{1,0:T(8,128)S(1)}, f32[128,256]{1,0:T(8,128)}, u32[]{:S(2)}) copy-start(f32[128,256]{1,0:T(8,128)} %get-tuple-element.4) | copy-start | bytes 393220
Sparse Core Ops, SparseCore 0:
  17.9 60.0 reduce-scatter.1
Sparse Core Ops, SparseCore 1:
  23.6 68.5 all-reduce.2
where the time goes:
time: 112 us
  waiting for transfers between devices  54.4 us (49%)
  blocking collectives  20.9 us (19%)
  between operations  15.5 us (14%)
  matrix products  10.6 us (9%)
  other arithmetic  5.74 us (5%)
  local copies, waits for them, and re-layouts  4.24 us (4%)
    reduce_scatter x1, waiting for transfers between devices, shards(): lax.psum_scatter(item_part, 'group', scatter_dimension=0, tiled=True)  54.4 us
    all_gather x1, blocking collectives, shards(): new_items = lax.all_gather(fresh_share, 'group', axis=0, tiled=True)  20.9 us
    dot_general x1, matrix products, shards(): jnp.dot(rating_errors, item_factors, preferred_element_type=jnp.float32)  4.76 us
    convert_element_type x3, other arithmetic, advance(): return (factors.astype(jnp.float32) + rate * gradient).astype(jnp.bfloat16)  4.4 us
    unnamed x15, local copies, waits for them, and re-layouts  3.49 us
    dot_general x2, matrix products, residual_of(): lax.dot_general(row_factors, column_factors, (((1,), (1,)), ((), ())), pr...  2.34 us
  transfers between devices with their start and end apart: 2, of which 1 were waited for; matrix products, arithmetic and copies ran while one was open for 6% of the time, Pallas kernels for 0%

commit v1 on v0

--- a/solution.py
+++ b/solution.py
@@ -51,7 +51,20 @@
     fresh_share = advance(
         own_share(item_factors, group_count, group_position), item_share, step_items
     )
-    new_items = lax.all_gather(fresh_share, "group", axis=0, tiled=True)
+    q_next, p_next, plain = (lax.axis_size("group"), lax.axis_index("group"), fresh_share.shape[0])
+    part_now, n_now = (fresh_share, 1)
+    while n_now < q_next:
+        part_now = jnp.concatenate(
+            [
+                part_now,
+                lax.ppermute(
+                    part_now, "group", [(idx, (idx - n_now) % q_next) for idx in range(q_next)]
+                ),
+            ],
+            axis=0,
+        )
+        n_now = 2 * n_now
+    new_items = jnp.roll(part_now, p_next * plain, axis=0)
     user_grad, tag_grad = lax.psum((user_part, tag_part), "loop")
     new_users = advance(user_factors, user_grad, step_users)
     new_tags = advance(tag_factors, tag_grad, step_tags)

time: 112 us -> 119 us (1.062)
  blocking collectives: 20.9 us -> 0 us
  waiting for transfers between devices: 54.4 us -> 75 us
  starting transfers between devices: 0.08 us -> 7 us
    all_gather x1 -> x0, blocking collectives: 20.9 us -> none  [shards(): new_items = lax.all_gather(fresh_share, 'group', axis=0, tiled=True)]
    ppermute x0 -> x4, waiting for transfers between devices: none -> 20.5 us  [shards(): lax.ppermute(part_now, 'group', [(idx, (idx - n_now) % q_next) for idx in...]
    ppermute x0 -> x4, starting transfers between devices: none -> 6.92 us  [shards(): lax.ppermute(part_now, 'group', [(idx, (idx - n_now) % q_next) for idx in...]
    convert_element_type x3 -> x2, other arithmetic: 4.4 us -> 3.55 us  [advance(): return (factors.astype(jnp.float32) + rate * gradient).astype(jnp.bfloat16)]
    unnamed x15 -> x22, local copies, waits for them, and re-layouts: 3.49 us -> 2.77 us
  transfers between devices with their start and end apart: 2 -> 6, of which waited for: 1 -> 5; matrix products, arithmetic and copies ran while one was open for 6% -> 6% of each run, Pallas kernels for 0% -> 0%
where the time goes in v1:
time: 119 us; the launch traced here: 118 us
  waiting for transfers between devices  75 us (63%)
  between operations  15.6 us (13%)
  matrix products  10.6 us (9%)
  starting transfers between devices  7 us (6%)
  other arithmetic  5.78 us (5%)
  local copies, waits for them, and re-layouts  4.37 us (4%)
    reduce_scatter x1, waiting for transfers between devices, shards(): lax.psum_scatter(item_part, 'group', scatter_dimension=0, tiled=True)  54.4 us
    ppermute x4, waiting for transfers between devices, shards(): lax.ppermute(part_now, 'group', [(idx, (idx - n_now) % q_next) for idx in...  20.5 us
    ppermute x4, starting transfers between devices, shards(): lax.ppermute(part_now, 'group', [(idx, (idx - n_now) % q_next) for idx in...  6.92 us
    dot_general x1, matrix products, shards(): jnp.dot(rating_errors, item_factors, preferred_element_type=jnp.float32)  4.78 us
    convert_element_type x2, other arithmetic, advance(): return (factors.astype(jnp.float32) + rate * gradient).astype(jnp.bfloat16)  3.55 us
    unnamed x22, local copies, waits for them, and re-layouts  2.77 us
  transfers between devices with their start and end apart: 6, of which 5 were waited for; matrix products, arithmetic and copies ran while one was open for 6% of the time, Pallas kernels for 0%

profile of v1, /device:TPU:0, one launch (start us, length us, event | category | flops | bytes accessed | tf_op | source)
XLA Modules:
  0.0 118.3 jit_solution(6647611687941753158)
XLA Ops:
  8.0 0.0 reduce-scatter.2.cloned.1.call-start
  8.0 0.7 convert_element_type.38
  8.7 0.1 copy.10
  8.8 0.7 convert_bitcast_fusion
  9.5 0.1 broadcast_bitcast_fusion
  9.5 0.0 copy-start
  9.5 0.0 copy-start.1
  9.5 0.0 copy-start.2
  9.5 0.6 mul.50
  10.2 0.4 copy-done
  10.6 0.3 copy-done.1
  10.9 1.3 %copy-done.2 = bf16[2048,1024]{1,0:T(8,128)(2,1)S(1)} copy-done((bf16[2048,1024]{1,0:T(8,128)(2,1)S(1)}, bf16[2048,1024]{1,0:T(8,128)(2,1)}, u32[]{:S(2)}) %copy-start.2) | copy-done | bytes 4194328
  12.2 2.0 %fusion = bf16[2048,1024]{1,0:T(8,128)(2,1)S(1)} fusion(f32[256,8,8,128]{3,2,1,0:T(8,128)S(1)} %bitcast.22, bf16[2048,1024]{1,0:T(8,128)(2,1)S(1)} %copy-done.2, bf16[2048,256]{1,0:T(8,128)(2,1)S(1)} %copy-done.1, bf16[1024,256]{1,0:T(8,128)(2,1)S(1)} %copy-done), kind=kOutput, calls=%fused_computation.1 | convolution fusion | flops 1082130432 | bytes 18350080 | tf_op jit(solution)/shard_map/dot_general | solution.py:19
  14.3 0.0 copy-start.3
  14.3 0.0 copy-start.4
  14.3 0.0 copy-start.5
  14.3 1.3 %fusion.4 = f32[1024,256]{1,0:T(8,128)S(1)} fusion(bf16[2048,1024]{1,0:T(8,128)(2,1)S(1)} %fusion, bf16[2048,256]{1,0:T(8,128)(2,1)S(1)} %copy-done.1), kind=kOutput, calls=%fused_computation.26 | convolution fusion | flops 1073741824 | bytes 6291456 | tf_op jit(solution)/shard_map/dot_general | solution.py:26
  15.6 0.6 copy-done.3
  16.2 0.0 copy-done.4
  16.2 0.0 copy-done.5
  16.2 0.3 fusion.2
  16.5 1.2 %convolution_add_fusion = f32[1024,256]{1,0:T(8,128)} fusion(f32[1024,256]{1,0:T(8,128)S(1)} %fusion.4, bf16[1024,128]{1,0:T(8,128)(2,1)S(1)} %fusion.2, bf16[128,256]{1,0:T(8,128)(2,1)S(1)} %copy-done.4), kind=kOutput, calls=%fused_computation.3 | convolution fusion | flops 67371008 | bytes 2424832 | tf_op jit(solution)/shard_map/dot_general | solution.py:43
  17.8 0.0 reduce-scatter.2.cloned.1.call-update
  17.8 0.0 all-reduce.3.cloned.1.call-start
  17.9 0.9 fusion.5
  18.8 4.8 %fusion.3 = f32[2048,256]{1,0:T(8,128)} fusion(bf16[2048,1024]{1,0:T(8,128)(2,1)} %copy-done.3, bf16[1024,256]{1,0:T(8,128)(2,1)S(1)} %copy-done), kind=kOutput, calls=%fused_computation.25 | convolution fusion | flops 1073741824 | bytes 6815744 | tf_op jit(solution)/shard_map/dot_general | solution.py:46
  23.5 0.0 all-reduce.3.cloned.1.call-update
  23.6 54.4 %reduce-scatter.2.cloned.1.call-done = f32[64,256]{1,0:T(8,128)} async-done(((f32[1024,256]{1,0:T(8,128)}), f32[64,256]{1,0:T(8,128)}) %reduce-scatter.2.cloned.1.call-update) | async-done | bytes 65552 | tf_op jit(solution)/shard_map/reduce_scatter | solution.py:48
  78.0 0.9 constant_dynamic-update-slice_fusion.9
  78.8 0.2 collective-permute-start
  79.0 1.6 %collective-permute-done = bf16[64,256]{1,0:T(8,128)(2,1)S(1)} collective-permute-done((bf16[64,256]{1,0:T(8,128)(2,1)S(1)}, bf16[64,256]{1,0:T(8,128)(2,1)S(1)}, u32[]{:S(2)}, u32[]{:S(2)}) %collective-permute-start) | collective-permute-done | bytes 32800 | tf_op jit(solution)/shard_map/ppermute | solution.py:60
  80.6 2.2 %collective-permute-start.1 = (bf16[128,256]{1,0:T(8,128)(2,1)S(1)}, bf16[128,256]{1,0:T(8,128)(2,1)S(1)}, u32[]{:S(2)}, u32[]{:S(2)}) collective-permute-start(bf16[128,256]{1,0:T(8,128)(2,1)S(1)} %pad_maximum_fusion.2), channel_id=1, source_target_pairs={{0,28},{2,30},{4,0},{6,2},{8,4},{10,6},{12,8},{14,10},{16,12},{18,... | collective-permute-start | bytes 196616 | tf_op jit(solution)/shard_map/ppermute | solution.py:60
  82.9 2.0 %collective-permute-done.1 = bf16[128,256]{1,0:T(8,128)(2,1)S(1)} collective-permute-done((bf16[128,256]{1,0:T(8,128)(2,1)S(1)}, bf16[128,256]{1,0:T(8,128)(2,1)S(1)}, u32[]{:S(2)}, u32[]{:S(2)}) %collective-permute-start.1) | collective-permute-done | bytes 65568 | tf_op jit(solution)/shard_map/ppermute | solution.py:60
  84.9 2.5 %collective-permute-start.2 = (bf16[256,256]{1,0:T(8,128)(2,1)S(1)}, bf16[256,256]{1,0:T(8,128)(2,1)S(1)}, u32[]{:S(2)}, u32[]{:S(2)}) collective-permute-start(bf16[256,256]{1,0:T(8,128)(2,1)S(1)} %pad_maximum_fusion.1), channel_id=1, source_target_pairs={{0,24},{2,26},{4,28},{6,30},{8,0},{10,2},{12,4},{14,6},{16,8},{18,... | collective-permute-start | bytes 393224 | tf_op jit(solution)/shard_map/ppermute | solution.py:60
  87.4 3.6 %collective-permute-done.2 = bf16[256,256]{1,0:T(8,128)(2,1)S(1)} collective-permute-done((bf16[256,256]{1,0:T(8,128)(2,1)S(1)}, bf16[256,256]{1,0:T(8,128)(2,1)S(1)}, u32[]{:S(2)}, u32[]{:S(2)}) %collective-permute-start.2) | collective-permute-done | bytes 131104 | tf_op jit(solution)/shard_map/ppermute | solution.py:60
  91.0 2.0 %collective-permute-start.3 = (bf16[512,256]{1,0:T(8,128)(2,1)S(1)}, bf16[512,256]{1,0:T(8,128)(2,1)S(1)}, u32[]{:S(2)}, u32[]{:S(2)}) collective-permute-start(bf16[512,256]{1,0:T(8,128)(2,1)S(1)} %pad_maximum_fusion), channel_id=1, source_target_pairs={{0,16},{2,18},{4,20},{6,22},{8,24},{10,26},{12,28},{14,30},{16,0},... | collective-permute-start | bytes 786440 | tf_op jit(solution)/shard_map/ppermute | solution.py:60
  93.0 13.3 %collective-permute-done.3 = bf16[512,256]{1,0:T(8,128)(2,1)S(1)} collective-permute-done((bf16[512,256]{1,0:T(8,128)(2,1)S(1)}, bf16[512,256]{1,0:T(8,128)(2,1)S(1)}, u32[]{:S(2)}, u32[]{:S(2)}) %collective-permute-start.3) | collective-permute-done | bytes 262176 | tf_op jit(solution)/shard_map/ppermute | solution.py:60
  106.5 0.8 constant_dynamic-slice_fusion
  107.3 0.0 all-reduce.3.cloned.1.call-done
  107.3 0.0 copy-start.6
  107.3 2.9 %add_convert_fusion = bf16[2048,256]{1,0:T(8,128)(2,1)} fusion(f32[2048,256]{1,0:T(8,128)} %get-tuple-element.3, bf16[2048,256]{1,0:T(8,128)(2,1)S(1)} %copy-done.1), kind=kLoop, calls=%fused_computation.2 | loop fusion | flops 2097152 | bytes 4194304 | tf_op jit(solution)/shard_map/convert_element_type | solution.py:32
  110.2 0.0 copy-done.6
  110.2 0.7 add_convert_fusion.1
  (12 shorter events, 0.1 us)
Async XLA Ops:
  8.0 70.0 %reduce-scatter.2.cloned.1.call-start = ((), (), s32[]{:S(2)}) async-start(), calls=%async_computation.1 | async-start | bytes 1114112 | tf_op jit(solution)/shard_map/reduce_scatter | solution.py:48
  9.5 1.0 copy-start
  9.5 1.4 %copy-start.1 = (bf16[2048,256]{1,0:T(8,128)(2,1)S(1)}, bf16[2048,256]{1,0:T(8,128)(2,1)}, u32[]{:S(2)}) copy-start(bf16[2048,256]{1,0:T(8,128)(2,1)} %param.7) | copy-start | bytes 3145732
  9.5 2.7 %copy-start.2 = (bf16[2048,1024]{1,0:T(8,128)(2,1)S(1)}, bf16[2048,1024]{1,0:T(8,128)(2,1)}, u32[]{:S(2)}) copy-start(bf16[2048,1024]{1,0:T(8,128)(2,1)} %param.10) | copy-start | bytes 12582916
  14.3 1.9 %copy-start.3 = (bf16[2048,1024]{1,0:T(8,128)(2,1)}, bf16[2048,1024]{1,0:T(8,128)(2,1)S(1)}, u32[]{:S(2)}) copy-start(bf16[2048,1024]{1,0:T(8,128)(2,1)S(1)} %fusion) | copy-start | bytes 12582916
  14.3 1.9 %copy-start.4 = (bf16[128,256]{1,0:T(8,128)(2,1)S(1)}, bf16[128,256]{1,0:T(8,128)(2,1)}, u32[]{:S(2)}) copy-start(bf16[128,256]{1,0:T(8,128)(2,1)} %param.9) | copy-start | bytes 196612
  14.3 1.9 %copy-start.5 = (bf16[1024,128]{1,0:T(8,128)(2,1)S(1)}, bf16[1024,128]{1,0:T(8,128)(2,1)}, u32[]{:S(2)}) copy-start(bf16[1024,128]{1,0:T(8,128)(2,1)} %param.12) | copy-start | bytes 786436
  17.8 89.5 %all-reduce.3.cloned.1.call-start = ((), (), s32[]{:S(2)}) async-start(), calls=%async_computation.2 | async-start | bytes 4456448 | tf_op jit(solution)/shard_map/psum | solution.py:68
  78.8 1.8 %collective-permute-start = (bf16[64,256]{1,0:T(8,128)(2,1)S(1)}, bf16[64,256]{1,0:T(8,128)(2,1)S(1)}, u32[]{:S(2)}, u32[]{:S(2)}) collective-permute-start(bf16[64,256]{1,0:T(8,128)(2,1)S(1)} %get-tuple-element.6), channel_id=1, source_target_pairs={{0,30},{2,0},{4,2},{6,4},{8,6},{10,8},{12,10},{14,12},{16,14},{18,... | collective-permute-start | bytes 98312 | tf_op jit(solution)/shard_map/ppermute | solution.py:60
  80.6 4.3 %collective-permute-start.1 = (bf16[128,256]{1,0:T(8,128)(2,1)S(1)}, bf16[128,256]{1,0:T(8,128)(2,1)S(1)}, u32[]{:S(2)}, u32[]{:S(2)}) collective-permute-start(bf16[128,256]{1,0:T(8,128)(2,1)S(1)} %pad_maximum_fusion.2), channel_id=1, source_target_pairs={{0,28},{2,30},{4,0},{6,2},{8,4},{10,6},{12,8},{14,10},{16,12},{18,... | collective-permute-start | bytes 196616 | tf_op jit(solution)/shard_map/ppermute | solution.py:60
  84.9 6.1 %collective-permute-start.2 = (bf16[256,256]{1,0:T(8,128)(2,1)S(1)}, bf16[256,256]{1,0:T(8,128)(2,1)S(1)}, u32[]{:S(2)}, u32[]{:S(2)}) collective-permute-start(bf16[256,256]{1,0:T(8,128)(2,1)S(1)} %pad_maximum_fusion.1), channel_id=1, source_target_pairs={{0,24},{2,26},{4,28},{6,30},{8,0},{10,2},{12,4},{14,6},{16,8},{18,... | collective-permute-start | bytes 393224 | tf_op jit(solution)/shard_map/ppermute | solution.py:60
  91.0 15.4 %collective-permute-start.3 = (bf16[512,256]{1,0:T(8,128)(2,1)S(1)}, bf16[512,256]{1,0:T(8,128)(2,1)S(1)}, u32[]{:S(2)}, u32[]{:S(2)}) collective-permute-start(bf16[512,256]{1,0:T(8,128)(2,1)S(1)} %pad_maximum_fusion), channel_id=1, source_target_pairs={{0,16},{2,18},{4,20},{6,22},{8,24},{10,26},{12,28},{14,30},{16,0},... | collective-permute-start | bytes 786440 | tf_op jit(solution)/shard_map/ppermute | solution.py:60
  107.3 2.9 %copy-start.6 = (f32[128,256]{1,0:T(8,128)S(1)}, f32[128,256]{1,0:T(8,128)}, u32[]{:S(2)}) copy-start(f32[128,256]{1,0:T(8,128)} %get-tuple-element.4) | copy-start | bytes 393220
Sparse Core Ops, SparseCore 0:
  17.9 60.0 reduce-scatter.1
Sparse Core Ops, SparseCore 1:
  23.7 68.5 all-reduce.2
